TPU v7x, 512 devices: a whole 4x4x16 slice. The times are simulated.
512 devices in a mesh: dp: 64 (over z, y_lo, core), expert: 8 (over y_hi, x).
Axes of the slice: x: 4, y: 4 (y_hi: 2, y_lo: 2; y = y_hi * 2 + y_lo), z: 16, core: 2. Of those that a mesh axis runs over, the one named last changes fastest.
Arguments:
- inputs: bfloat16 [256, 3072], P('dp', 'expert'), may hold values from -6 to 6
- routes: int32 [256, 2], P('dp'), may hold values from 0 to 7, all different within a row; in each aligned block of 4 rows (0 to 3, 4 to 7, ...) at most 2 rows name the same one
- combine: float32 [256, 2], P('dp'), may hold values from 0.1 to 1
- cotangent: bfloat16 [256, 3072], P('dp', 'expert'), may hold values from -6 to 6
- w_gate: bfloat16 [8, 3072, 8192], P('expert', None, 'dp'), may hold values from -0.109375 to 0.109375
- w_up: bfloat16 [8, 3072, 8192], P('expert', None, 'dp'), may hold values from -0.109375 to 0.109375
- w_down: bfloat16 [8, 8192, 3072], P('expert', 'dp'), may hold values from -0.0625 to 0.0625
Outputs:
- input_grad: bfloat16 [256, 3072], P('dp', 'expert')
- gate_grad: bfloat16 [8, 3072, 8192], P('expert', None, 'dp')
- up_grad: bfloat16 [8, 3072, 8192], P('expert', None, 'dp')
- down_grad: bfloat16 [8, 8192, 3072], P('expert', 'dp')
Inputs may be any that keep to these rules, and one draw needn't show every extreme that they name: `routes`: each token names two different experts. Among the tokens of one index of dp no expert is named more than 2 times, a bound that some block reaches there.
All inputs are finite; a program needn't handle non-finite values.
Results may differ from a plain program's by a relative error of at most 0.0065.
Values may be sent and summed in bfloat16 or wider, within the bound.
No kernel may reach another device: no remote copies, remote signals or barrier semaphores. Data moves between devices by JAX's collectives and lax.ppermute only.
A program may use at most 64 MiB of HBM per device.

v0:
```python
import jax
import jax.numpy as jnp
from jax import lax
from jax.sharding import PartitionSpec as P

MOST = 2


def forward_part(all_inputs, w_gate, w_up):
    gate_pre = jnp.einsum("rld,ldf->rlf", all_inputs, w_gate, preferred_element_type=jnp.float32)
    up_pre = jnp.einsum("rld,ldf->rlf", all_inputs, w_up, preferred_element_type=jnp.float32)
    gate_sig = jax.nn.sigmoid(gate_pre)
    activated = gate_pre * gate_sig
    hidden = (activated * up_pre).astype(jnp.bfloat16)
    return (gate_pre, up_pre, gate_sig, activated, hidden)


def per_device(inputs, routes, combine, cotangent, w_gate, w_up, w_down):
    local_experts = w_gate.shape[0]
    expert_count = local_experts * lax.axis_size("expert")
    slot_count = MOST
    width_part = inputs.shape[1]
    routes_flat = routes.reshape(-1)
    onehot = (routes_flat[:, None] == jnp.arange(expert_count, dtype=jnp.int32)[None, :]).astype(
        jnp.int32
    )
    before = jnp.cumsum(onehot, axis=0) - onehot
    slot_index = jnp.sum(before * onehot, axis=1)
    column = slot_index * expert_count + routes_flat
    placer = column[:, None] == jnp.arange(slot_count * expert_count, dtype=jnp.int32)[None, :]
    placer_half = placer.astype(jnp.bfloat16)
    repeated = jnp.repeat(inputs, 2, axis=0)
    scaled = (
        combine.reshape(-1)[:, None] * jnp.repeat(cotangent, 2, axis=0).astype(jnp.float32)
    ).astype(jnp.bfloat16)
    sent_inputs = jnp.einsum(
        "jc,jd->cd", placer_half, repeated, preferred_element_type=jnp.float32
    ).astype(jnp.bfloat16)
    sent_grads = jnp.einsum(
        "jc,jd->cd", placer_half, scaled, preferred_element_type=jnp.float32
    ).astype(jnp.bfloat16)
    sent_inputs = sent_inputs.reshape(slot_count, expert_count, width_part)
    sent_grads = sent_grads.reshape(slot_count, expert_count, width_part)
    expert_inputs, expert_grads = (
        lax.all_to_all(sent_inputs, "expert", split_axis=1, concat_axis=2, tiled=True),
        lax.all_to_all(sent_grads, "expert", split_axis=1, concat_axis=2, tiled=True),
    )
    all_inputs, all_grads = (
        lax.all_gather(expert_inputs, "dp", axis=0, tiled=True),
        lax.all_gather(expert_grads, "dp", axis=0, tiled=True),
    )
    gate_pre, up_pre, gate_sig, activated, hidden = forward_part(all_inputs, w_gate, w_up)
    hidden_delta = jnp.einsum("rld,lfd->rlf", all_grads, w_down, preferred_element_type=jnp.float32)
    down_grad = jnp.einsum(
        "rlf,rld->lfd", hidden, all_grads, preferred_element_type=jnp.float32
    ).astype(jnp.bfloat16)
    gate_delta = (hidden_delta * up_pre * gate_sig * (1.0 + gate_pre * (1.0 - gate_sig))).astype(
        jnp.bfloat16
    )
    up_delta = (hidden_delta * activated).astype(jnp.bfloat16)
    gate_grad = jnp.einsum(
        "rld,rlf->ldf", all_inputs, gate_delta, preferred_element_type=jnp.float32
    ).astype(jnp.bfloat16)
    up_grad = jnp.einsum(
        "rld,rlf->ldf", all_inputs, up_delta, preferred_element_type=jnp.float32
    ).astype(jnp.bfloat16)
    from_gate = jnp.einsum("rlf,ldf->rld", gate_delta, w_gate, preferred_element_type=jnp.float32)
    from_up = jnp.einsum("rlf,ldf->rld", up_delta, w_up, preferred_element_type=jnp.float32)
    own_rows = lax.psum_scatter(from_gate + from_up, "dp", scatter_dimension=0, tiled=True)
    back_rows = lax.all_to_all(own_rows, "expert", split_axis=2, concat_axis=1, tiled=True)
    back_flat = back_rows.reshape(slot_count * expert_count, width_part)
    assign_grad = jnp.dot(placer.astype(jnp.float32), back_flat, precision=lax.Precision.HIGHEST)
    input_grad = jnp.sum(assign_grad.reshape(inputs.shape[0], 2, width_part), axis=1).astype(
        jnp.bfloat16
    )
    return (input_grad, gate_grad, up_grad, down_grad)


def solution(mesh):
    placed = (
        P("dp", "expert"),
        P("dp", None),
        P("dp", None),
        P("dp", "expert"),
        P("expert", None, "dp"),
        P("expert", None, "dp"),
        P("expert", "dp", None),
    )
    return jax.shard_map(
        per_device,
        mesh=mesh,
        in_specs=placed,
        out_specs=(
            P("dp", "expert"),
            P("expert", None, "dp"),
            P("expert", None, "dp"),
            P("expert", "dp", None),
        ),
        check_vma=False,
    )
```

profile of v0, /device:TPU:1, one launch (start us, length us, event | category | flops | bytes accessed | tf_op | source)
XLA Modules:
  0.0 658.0 jit_solution(9490560236936488608)
XLA Ops:
  7.2 0.8 copy.37
  8.4 0.7 broadcast_in_dim.10
  9.4 0.6 copy.43
  10.0 7.5 %all-to-all-start.1 = ((bf16[2,8,384]{2,0,1:T(2,128)(2,1)}), bf16[2,8,384]{2,0,1:T(2,128)(2,1)S(1)}, u32[]{:S(2)}, u32[]{:S(2)}) async-start(bf16[2,8,384]{2,0,1:T(2,128)(2,1)} %copy.43), calls=%async_computation.1 | async-start | bytes 24576 | tf_op jit(solution)/shard_map/all_to_all | solution.py:45
  17.5 0.8 copy.40
  18.3 0.7 broadcast_in_dim.4
  19.3 0.6 copy.41
  19.9 4.1 all-to-all-done.1
  24.0 3.3 all-to-all-start
  27.4 6.4 all-to-all-done
  33.9 76.2 %all_gather.6 = bf16[128,1,3072]{2,1,0:T(2,128)(2,1)S(1)} all-gather(bf16[2,1,3072]{2,1,0:T(2,128)(2,1)S(1)} %copy.42), channel_id=1, replica_groups=mesh['dp'=64,'expert'=8] {'dp'}, dimensions={0}, use_global_device_ids=true | all-gather | bytes 798720 | tf_op jit(solution)/shard_map/all_gather | solution.py:50
  110.1 63.8 %all_gather.7 = bf16[128,1,3072]{2,1,0:T(2,128)(2,1)S(1)} all-gather(bf16[2,1,3072]{2,1,0:T(2,128)(2,1)S(1)} %copy.44), channel_id=1, replica_groups=mesh['dp'=64,'expert'=8] {'dp'}, dimensions={0}, use_global_device_ids=true | all-gather | bytes 798720 | tf_op jit(solution)/shard_map/all_gather | solution.py:49
  174.5 0.5 copy-done.1
  175.3 0.4 fusion.21
  175.8 0.4 fusion.12
  176.1 1.5 fusion
  177.9 1.3 dynamic-slice
  179.8 1.3 fusion.2
  181.1 1.3 fusion.3
  182.4 429.8 %all-reduce.3.cloned.1.call-done = f32[128,1,3072]{2,0,1:T(8,128)} async-done(((f32[128,1,3072]{2,0,1:T(8,128)}), f32[128,1,3072]{2,0,1:T(8,128)}) %all-reduce.3.cloned.1.call-update) | async-done | bytes 1572880
  612.2 0.9 constant_dynamic-slice_fusion
  613.1 1.6 copy.45
  614.7 0.5 broadcast.50
  615.2 14.8 %reduce = f32[3072,2]{1,0:T(8,128)} reduce(f32[3072,1,2]{2,1,0:T(1,128)S(1)} %bitcast.92, f32[]{:T(128)} %broadcast.50), dimensions={1}, to_apply=%bitcast.79.reduce_sub_computation | reduce | bytes 49156
  630.0 3.0 reshape.131
  633.1 6.2 all-to-all-start.2
  639.2 1.3 fusion.1
  640.5 5.3 all-to-all-done.2
  645.8 0.7 reduce.1
  646.5 2.5 reshape.132
  649.1 1.3 copy.46
  650.4 0.8 convolution_reduce_fusion
  (26 shorter events, 2.3 us)
Async XLA Ops:
  7.2 166.9 %copy-start = (bf16[1,3072,128]{2,1,0:T(8,128)(2,1)S(1)}, bf16[1,3072,128]{2,1,0:T(8,128)(2,1)}, u32[]{:S(2)}) copy-start(bf16[1,3072,128]{2,1,0:T(8,128)(2,1)} %param.11) | copy-start | bytes 2359300
  10.0 14.0 %all-to-all-start.1 = ((bf16[2,8,384]{2,0,1:T(2,128)(2,1)}), bf16[2,8,384]{2,0,1:T(2,128)(2,1)S(1)}, u32[]{:S(2)}, u32[]{:S(2)}) async-start(bf16[2,8,384]{2,0,1:T(2,128)(2,1)} %copy.43), calls=%async_computation.1 | async-start | bytes 24576 | tf_op jit(solution)/shard_map/all_to_all | solution.py:45
  24.0 9.8 %all-to-all-start = ((bf16[2,8,384]{2,0,1:T(2,128)(2,1)}), bf16[2,8,384]{2,0,1:T(2,128)(2,1)S(1)}, u32[]{:S(2)}, u32[]{:S(2)}) async-start(bf16[2,8,384]{2,0,1:T(2,128)(2,1)} %copy.41), calls=%async_computation | async-start | bytes 24576 | tf_op jit(solution)/shard_map/all_to_all | solution.py:46
  27.4 584.8 %all-reduce.3.cloned.1.call-start = ((), (), s32[]{:S(2)}) async-start(), calls=%async_computation.3 | async-start | bytes 3145728
  173.8 1.1 copy-start.1
  174.1 1.2 copy-start.2
  633.1 12.7 %all-to-all-start.2 = ((f32[8,1,768]{2,1,0:T(1,128)}), f32[8,1,768]{2,1,0:T(1,128)S(1)}, u32[]{:S(2)}, u32[]{:S(2)}) async-start(f32[8,1,768]{2,1,0:T(1,128)} %reshape.131), calls=%async_computation.2 | async-start | bytes 49152 | tf_op jit(solution)/shard_map/all_to_all | solution.py:70
Sparse Core Ops, SparseCore 0:
  177.8 434.3 all-reduce.2
where the time goes:
time: 659 us; the launch traced here: 658 us
  waiting for transfers between devices  446 us (68%)
  blocking collectives  140 us (21%)
  starting transfers between devices  17 us (3%)
  local copies, waits for them, and re-layouts  16.5 us (3%)
  other arithmetic  15.8 us (2%)
  between operations  14.8 us (2%)
  matrix products  8.23 us (1%)
    unnamed x2, waiting for transfers between devices  430 us
    all_gather x1, blocking collectives, per_device(): lax.all_gather(expert_grads, 'dp', axis=0, tiled=True)  76.2 us
    all_gather x1, blocking collectives, per_device(): lax.all_gather(expert_inputs, 'dp', axis=0, tiled=True)  63.8 us
    unnamed x1, other arithmetic  14.8 us
  transfers between devices with their start and end apart: 4, of which 4 were waited for; matrix products, arithmetic and copies ran while one was open for 1% of the time, Pallas kernels for 0%

commit v1 on v0

--- a/solution.py
+++ b/solution.py
@@ -67,7 +67,12 @@
     from_gate = jnp.einsum("rlf,ldf->rld", gate_delta, w_gate, preferred_element_type=jnp.float32)
     from_up = jnp.einsum("rlf,ldf->rld", up_delta, w_up, preferred_element_type=jnp.float32)
     own_rows = lax.psum_scatter(from_gate + from_up, "dp", scatter_dimension=0, tiled=True)
-    back_rows = lax.all_to_all(own_rows, "expert", split_axis=2, concat_axis=1, tiled=True)
+    back_rows = jnp.concatenate(
+        lax.all_to_all(
+            jnp.stack(jnp.split(own_rows, lax.axis_size("expert"), axis=2)), "expert", 0, 0
+        ),
+        axis=1,
+    )
     back_flat = back_rows.reshape(slot_count * expert_count, width_part)
     assign_grad = jnp.dot(placer.astype(jnp.float32), back_flat, precision=lax.Precision.HIGHEST)
     input_grad = jnp.sum(assign_grad.reshape(inputs.shape[0], 2, width_part), axis=1).astype(

time: 659 us -> 645 us (0.979)
  other arithmetic: 15.8 us -> 0.3 us
    unnamed x1 -> x0, other arithmetic: 14.8 us -> none
    unnamed x14 -> x17, local copies, waits for them, and re-layouts: 10.6 us -> 13.2 us
where the time goes in v1:
time: 645 us; the launch traced here: 644 us
  waiting for transfers between devices  446 us (69%)
  blocking collectives  140 us (22%)
  local copies, waits for them, and re-layouts  17.6 us (3%)
  starting transfers between devices  17 us (3%)
  between operations  14.8 us (2%)
  matrix products  8.24 us (1%)
    unnamed x2, waiting for transfers between devices  430 us
    all_gather x1, blocking collectives, per_device(): lax.all_gather(expert_grads, 'dp', axis=0, tiled=True)  76.2 us
    all_gather x1, blocking collectives, per_device(): lax.all_gather(expert_inputs, 'dp', axis=0, tiled=True)  63.8 us
    unnamed x17, local copies, waits for them, and re-layouts  13.2 us
  transfers between devices with their start and end apart: 4, of which 4 were waited for; matrix products, arithmetic and copies ran while one was open for 1% of the time, Pallas kernels for 0%

profile of v1, /device:TPU:1, one launch (start us, length us, event | category | flops | bytes accessed | tf_op | source)
XLA Modules:
  0.0 643.5 jit_solution(12326835436212964745)
XLA Ops:
  7.2 0.8 copy.59
  8.4 0.7 broadcast_in_dim.10
  9.4 0.6 copy.65
  10.0 7.5 %all-to-all-start.1 = ((bf16[2,8,384]{2,0,1:T(2,128)(2,1)}), bf16[2,8,384]{2,0,1:T(2,128)(2,1)S(1)}, u32[]{:S(2)}, u32[]{:S(2)}) async-start(bf16[2,8,384]{2,0,1:T(2,128)(2,1)} %copy.65), calls=%async_computation.1 | async-start | bytes 24576 | tf_op jit(solution)/shard_map/all_to_all | solution.py:45
  17.5 0.8 copy.62
  18.3 0.7 broadcast_in_dim.4
  19.3 0.6 copy.63
  19.9 4.1 all-to-all-done.1
  24.0 3.3 all-to-all-start
  27.4 6.4 all-to-all-done
  33.9 76.2 %all_gather.6 = bf16[128,1,3072]{2,1,0:T(2,128)(2,1)S(1)} all-gather(bf16[2,1,3072]{2,1,0:T(2,128)(2,1)S(1)} %copy.64), channel_id=1, replica_groups=mesh['dp'=64,'expert'=8] {'dp'}, dimensions={0}, use_global_device_ids=true | all-gather | bytes 798720 | tf_op jit(solution)/shard_map/all_gather | solution.py:50
  110.1 63.8 %all_gather.7 = bf16[128,1,3072]{2,1,0:T(2,128)(2,1)S(1)} all-gather(bf16[2,1,3072]{2,1,0:T(2,128)(2,1)S(1)} %copy.66), channel_id=1, replica_groups=mesh['dp'=64,'expert'=8] {'dp'}, dimensions={0}, use_global_device_ids=true | all-gather | bytes 798720 | tf_op jit(solution)/shard_map/all_gather | solution.py:49
  174.5 0.5 copy-done.1
  175.3 0.4 fusion.21
  175.8 0.4 fusion.12
  176.1 1.5 fusion
  177.9 1.3 dynamic-slice
  179.8 1.3 fusion.2
  181.1 1.3 fusion.3
  182.4 429.8 %all-reduce.3.cloned.1.call-done = f32[128,1,3072]{2,0,1:T(8,128)} async-done(((f32[128,1,3072]{2,0,1:T(8,128)}), f32[128,1,3072]{2,0,1:T(8,128)}) %all-reduce.3.cloned.1.call-update) | async-done | bytes 1572880
  612.2 1.3 constant_dynamic-update-slice_fusion.7
  613.5 1.4 constant_dynamic-update-slice_fusion.6
  614.9 1.4 constant_dynamic-update-slice_fusion.5
  616.3 1.4 constant_dynamic-update-slice_fusion.4
  617.6 1.4 constant_dynamic-update-slice_fusion.3
  619.0 1.4 constant_dynamic-update-slice_fusion.2
  620.4 1.4 constant_dynamic-update-slice_fusion.1
  621.8 1.4 constant_dynamic-update-slice_fusion
  623.1 6.1 all-to-all-start.2
  629.3 1.3 fusion.1
  630.6 5.3 all-to-all-done.2
  635.9 0.8 convolution_reduce_fusion
  (25 shorter events, 2.3 us)
Async XLA Ops:
  7.2 166.9 %copy-start = (bf16[1,3072,128]{2,1,0:T(8,128)(2,1)S(1)}, bf16[1,3072,128]{2,1,0:T(8,128)(2,1)}, u32[]{:S(2)}) copy-start(bf16[1,3072,128]{2,1,0:T(8,128)(2,1)} %param.11) | copy-start | bytes 2359300
  10.0 14.0 %all-to-all-start.1 = ((bf16[2,8,384]{2,0,1:T(2,128)(2,1)}), bf16[2,8,384]{2,0,1:T(2,128)(2,1)S(1)}, u32[]{:S(2)}, u32[]{:S(2)}) async-start(bf16[2,8,384]{2,0,1:T(2,128)(2,1)} %copy.65), calls=%async_computation.1 | async-start | bytes 24576 | tf_op jit(solution)/shard_map/all_to_all | solution.py:45
  24.0 9.8 %all-to-all-start = ((bf16[2,8,384]{2,0,1:T(2,128)(2,1)}), bf16[2,8,384]{2,0,1:T(2,128)(2,1)S(1)}, u32[]{:S(2)}, u32[]{:S(2)}) async-start(bf16[2,8,384]{2,0,1:T(2,128)(2,1)} %copy.63), calls=%async_computation | async-start | bytes 24576 | tf_op jit(solution)/shard_map/all_to_all | solution.py:46
  27.4 584.8 %all-reduce.3.cloned.1.call-start = ((), (), s32[]{:S(2)}) async-start(), calls=%async_computation.3 | async-start | bytes 3145728
  173.8 1.1 copy-start.1
  174.1 1.2 copy-start.2
  623.1 12.7 %all-to-all-start.2 = ((f32[8,2,1,384]{3,1,2,0:T(2,128)}), f32[8,2,1,384]{3,1,2,0:T(2,128)S(1)}, u32[]{:S(2)}, u32[]{:S(2)}) async-start(f32[8,2,1,384]{3,1,2,0:T(2,128)} %constant_dynamic-update-slice_fusion), calls=%async_computation.2 | async-start | bytes 49152 | tf_op jit(solution)/shard_map/all_to_all | solution.py:71
Sparse Core Ops, SparseCore 0:
  177.8 434.3 all-reduce.2
